TPU v7x, 32 devices: a whole 2x2x4 slice. The times are simulated.
32 devices in a mesh: grp: 2 (over x), gx: 16 (over z, y, core).
Axes of the slice: x: 2, y: 2, z: 4, core: 2. Of those that a mesh axis runs over, the one named last changes fastest.
Arguments:
- e_forward: float32 [3, 256, 32, 256], P(None, ('grp', 'gx')), parts along dimension 1, may hold values from -6 to 6
- h_forward: float32 [3, 256, 32, 256], P(None, ('grp', 'gx')), parts along dimension 1, may hold values from -6 to 6
- p_forward: float32 [3, 256, 32, 256], P(None, ('grp', 'gx')), parts along dimension 1, may hold values from -6 to 6
- j_forward: float32 [3, 256, 32, 256], P(None, ('grp', 'gx')), parts along dimension 1, may hold values from -6 to 6
- e_adjoint: float32 [3, 256, 32, 256], P(None, ('grp', 'gx')), parts along dimension 1, may hold values from -6 to 6
- h_adjoint: float32 [3, 256, 32, 256], P(None, ('grp', 'gx')), parts along dimension 1, may hold values from -6 to 6
- p_adjoint: float32 [3, 256, 32, 256], P(None, ('grp', 'gx')), parts along dimension 1, may hold values from -6 to 6
- j_adjoint: float32 [3, 256, 32, 256], P(None, ('grp', 'gx')), parts along dimension 1, may hold values from -6 to 6
- design: float32 [32, 32, 256], P(('grp', 'gx')), parts along dimension 0, may hold values from 0 to 1
- source_amp: float32 [32, 3], P('grp'), parts along dimension 0, may hold values from -6 to 6
- source_cell: int32 [32], P('grp'), parts along dimension 0, may hold values from 0 to 1048575
- monitor_cell: int32 [32], P('grp'), parts along dimension 0, may hold values from 0 to 1048575
- slab_start: int32 [2], P('grp'), parts along dimension 0, may hold values from 8 to 15
- radius: int32 [2], P('grp'), parts along dimension 0, may hold values from 1 to 4
Outputs:
- e_forward_next: float32 [3, 256, 32, 256], P(None, ('grp', 'gx')), parts along dimension 1
- h_forward_next: float32 [3, 256, 32, 256], P(None, ('grp', 'gx')), parts along dimension 1
- e_adjoint_next: float32 [3, 256, 32, 256], P(None, ('grp', 'gx')), parts along dimension 1
- h_adjoint_next: float32 [3, 256, 32, 256], P(None, ('grp', 'gx')), parts along dimension 1
- design_grad: float32 [32, 32, 256], P(('grp', 'gx')), parts along dimension 0
There are 2 independent parts, one for each index of `grp`. A program takes and returns all parts, laid end to end along the dimension named above; each array names one. Nothing has to cross between parts.
Inputs may be any that keep to these rules, and one draw needn't show every extreme that they name: `slab_start`: the slab begins within planes 8 to 15 of the grid.
All inputs are finite; a program needn't handle non-finite values.
Results may differ from a plain program's by a relative error of at most 0.0003.
Values sent between devices are 32-bit elements; how exact they have to be, the bound alone decides.
No kernel may reach another device: no remote copies, remote signals or barrier semaphores. Data moves between devices by JAX's collectives and lax.ppermute only.
A program may use at most 128 MiB of HBM per device.

v0:
```python
import jax
import jax.numpy as jnp
from jax import lax
from jax.sharding import PartitionSpec as P

DT = 0.5
EPS_RANGE = 10.0
STRENGTH_BASE = 0.5
STRENGTH_RANGE = 3.0
DAMPING = 0.2
GAIN_FIELD = 0.25
HIGH = lax.Precision.HIGHEST


def passed_along(block, axis, distance):
    devices = range(lax.axis_size(axis))
    route = [(i - distance, i) for i in devices if i - distance in devices]
    return lax.ppermute(block, axis, route)


def band_matrix(count, radius):
    rows = jnp.arange(count, dtype=jnp.int32)
    dist = jnp.abs(rows[:, None] - rows[None, :])
    weights = jnp.maximum(radius + 1 - dist, 0).astype(jnp.float32)
    return weights / jnp.sum(weights, axis=1, keepdims=True)


def ahead(field, axis):
    count = field.shape[axis]
    rest = lax.slice_in_dim(field, 1, count, axis=axis)
    return jnp.concatenate([rest, jnp.zeros_like(lax.slice_in_dim(field, 0, 1, axis=axis))], axis)


def behind(field, axis):
    count = field.shape[axis]
    rest = lax.slice_in_dim(field, 0, count - 1, axis=axis)
    return jnp.concatenate([jnp.zeros_like(lax.slice_in_dim(field, 0, 1, axis=axis)), rest], axis)


def update_h(efield, hfield, upper):
    ex, ey, ez = (efield[0], efield[1], efield[2])
    ex_next = jnp.concatenate([ex[1:], upper[0][None]], 0)
    ey_next = jnp.concatenate([ey[1:], upper[1][None]], 0)
    curl_x = ahead(ez, 2) - ez - (ey_next - ey)
    curl_y = ex_next - ex - (ahead(ez, 1) - ez)
    curl_z = ahead(ey, 1) - ey - (ahead(ex, 2) - ex)
    return hfield - DT * jnp.stack([curl_x, curl_y, curl_z])


def update_e(efield, hnext, lower, jnext, permittivity, drive):
    hx, hy, hz = (hnext[0], hnext[1], hnext[2])
    hx_prev = jnp.concatenate([lower[0][None], hx[:-1]], 0)
    hy_prev = jnp.concatenate([lower[1][None], hy[:-1]], 0)
    curl_x = hz - behind(hz, 2) - (hy - hy_prev)
    curl_y = hx - hx_prev - (hz - behind(hz, 1))
    curl_z = hy - behind(hy, 1) - (hx - behind(hx, 2))
    curl = jnp.stack([curl_x, curl_y, curl_z])
    return efield + (DT / permittivity)[None] * (curl - jnext + drive)


def update_j(jfield, pfield, efield, strength):
    return ((1.0 - DAMPING * DT / 2.0) * jfield + DT * (strength[None] * efield - pfield)) / (
        1.0 + DAMPING * DT / 2.0
    )


def smooth(wx, wy, planes):
    inner = jnp.einsum("ax,zxy->zay", wx, planes, precision=HIGH)
    return jnp.einsum("zay,by->zab", inner, wy, precision=HIGH)


def smooth_adjoint(wx, wy, planes):
    inner = jnp.einsum("ax,zab->zxb", wx, planes, precision=HIGH)
    return jnp.einsum("zxb,by->zxy", inner, wy, precision=HIGH)


def locate(cells, first, depth, width_x, width_y):
    zz = cells // (width_x * width_y)
    rest = cells % (width_x * width_y)
    local = zz - first
    inside = ((local >= 0) & (local < depth)).astype(jnp.float32)
    return (jnp.clip(local, 0, depth - 1), rest // width_y, rest % width_y, inside)


def body(
    e_forward,
    h_forward,
    p_forward,
    j_forward,
    e_adjoint,
    h_adjoint,
    p_adjoint,
    j_adjoint,
    design,
    source_amp,
    source_cell,
    monitor_cell,
    slab_start,
    radius,
):
    index = lax.axis_index("gx")
    depth, width_x, width_y = (e_forward.shape[1], e_forward.shape[2], e_forward.shape[3])
    start = slab_start[0]
    wx = band_matrix(width_x, radius[0])
    wy = band_matrix(width_y, radius[0])
    upper = passed_along(
        jnp.stack([e_forward[0, 0], e_forward[1, 0], e_adjoint[0, 0], e_adjoint[1, 0]]), "gx", -1
    )
    hf = update_h(e_forward, h_forward, upper[0:2])
    ha = update_h(e_adjoint, h_adjoint, upper[2:4])
    gathered = lax.all_gather(design, "gx", axis=0, tiled=True)
    slab = gathered.shape[0]
    planes = index * depth + jnp.arange(depth, dtype=jnp.int32) - start
    valid = ((planes >= 0) & (planes < slab)).astype(jnp.float32)
    picked = jnp.take(gathered, jnp.clip(planes, 0, slab - 1), axis=0) * valid[:, None, None]
    density = smooth(wx, wy, picked)
    permittivity = 1.0 + EPS_RANGE * density
    strength = STRENGTH_BASE + STRENGTH_RANGE * density
    lower = passed_along(jnp.stack([hf[0, -1], hf[1, -1], ha[0, -1], ha[1, -1]]), "gx", 1)
    zs, xs, ys, inside_s = locate(source_cell, index * depth, depth, width_x, width_y)
    nsrc = zs.shape[0]
    comp = jnp.repeat(jnp.arange(3, dtype=jnp.int32), nsrc)
    drive = (
        jnp.zeros((3, depth, width_x, width_y), jnp.float32)
        .at[comp, jnp.tile(zs, 3), jnp.tile(xs, 3), jnp.tile(ys, 3)]
        .add((source_amp.T * inside_s[None, :]).reshape(-1))
    )
    zm, xm, ym, inside_m = locate(monitor_cell, index * depth, depth, width_x, width_y)
    count = jnp.zeros((depth, width_x, width_y), jnp.float32).at[zm, xm, ym].add(inside_m)
    drive_adj = count[None] * e_forward
    jf = update_j(j_forward, p_forward, e_forward, strength)
    ja = update_j(j_adjoint, p_adjoint, e_adjoint, strength)
    ef = update_e(e_forward, hf, lower[0:2], jf, permittivity, drive)
    ea = update_e(e_adjoint, ha, lower[2:4], ja, permittivity, drive_adj)
    intersection = jnp.sum(ea * (ef - e_forward + GAIN_FIELD * ef), axis=0)
    slots = jnp.arange(slab, dtype=jnp.int32)
    select = (planes[:, None] == slots[None, :]).astype(jnp.float32)
    returned = jnp.einsum("lo,lxy->oxy", select, intersection, precision=HIGH)
    own_intersection = lax.psum_scatter(returned, "gx", scatter_dimension=0, tiled=True)
    design_grad = smooth_adjoint(wx, wy, own_intersection)
    return (ef, hf, ea, ha, design_grad)


def solution(mesh):
    return jax.shard_map(
        body,
        mesh=mesh,
        in_specs=(
            P(None, ("grp", "gx"), None, None),
            P(None, ("grp", "gx"), None, None),
            P(None, ("grp", "gx"), None, None),
            P(None, ("grp", "gx"), None, None),
            P(None, ("grp", "gx"), None, None),
            P(None, ("grp", "gx"), None, None),
            P(None, ("grp", "gx"), None, None),
            P(None, ("grp", "gx"), None, None),
            P(("grp", "gx"), None, None),
            P("grp", None),
            P("grp"),
            P("grp"),
            P("grp"),
            P("grp"),
        ),
        out_specs=(
            P(None, ("grp", "gx"), None, None),
            P(None, ("grp", "gx"), None, None),
            P(None, ("grp", "gx"), None, None),
            P(None, ("grp", "gx"), None, None),
            P(("grp", "gx"), None, None),
        ),
        check_vma=False,
    )
```

profile of v0, /device:TPU:0, one launch (start us, length us, event | category | flops | bytes accessed | tf_op | source)
XLA Modules:
  0.0 142.5 jit_solution(9310592674110908171)
XLA Ops:
  7.2 0.9 slice_bitcast_fusion.25
  8.8 1.3 collective-permute-start
  12.1 1.9 %slice_bitcast_fusion.17 = (f32[7,32,256]{2,1,0:T(8,128)}, f32[7,32,256]{2,1,0:T(8,128)}) fusion(f32[3,8,32,256]{3,2,1,0:T(8,128)} %param.18), kind=kLoop, calls=%fused_computation.73 | loop fusion | bytes 917504 | tf_op jit(solution)/shard_map/slice | solution.py:43
  14.0 0.8 slice_bitcast_fusion.19
  16.6 0.8 slice.269
  22.5 25.4 %all_gather.3 = f32[16,32,256]{2,1,0:T(8,128)S(1)} all-gather(f32[1,32,256]{2,1,0:T(8,128)} %param.22), channel_id=1, replica_groups=mesh['grp'=2,'gx'=16] {'gx'}, dimensions={0}, use_global_device_ids=true | all-gather | bytes 557056 | tf_op jit(solution)/shard_map/all_gather | solution.py:111
  48.7 0.8 copy-done.11
  49.6 0.8 slice.274
  53.1 1.3 add_divide_fusion
  54.5 1.6 %scatter_fusion.1 = f32[8,32,256]{2,1,0:T(8,128)S(1)} fusion(f32[8,32,256]{2,1,0:T(8,128)S(1)} %broadcast_in_dim.23, s32[16]{0:T(128)S(1)} %fusion.56, f32[16]{0:T(128)S(1)} %get-tuple-element.8), kind=kCustom, calls=%fused_computation.2 | custom fusion | flops 16 | bytes 384 | tf_op jit(solution)/shard_map/scatter-add | solution.py:129
  56.1 0.9 copy-done.10
  57.2 0.9 copy-done.20
  58.3 0.9 slice_bitcast_fusion.13
  59.2 0.9 slice_bitcast_fusion.2
  61.0 0.9 copy-done.21
  62.2 2.3 %collective-permute-start.1 = (f32[4,32,256]{2,1,0:T(8,128)S(1)}, f32[4,32,256]{2,1,0:T(8,128)S(1)}, u32[]{:S(2)}, u32[]{:S(2)}) collective-permute-start(f32[4,32,256]{2,1,0:T(8,128)S(1)} %pad_maximum_fusion.1), channel_id=1, source_target_pairs={{0,1},{1,2},{2,3},{3,4},{4,5},{5,6},{6,7},{7,8},{8,9},{9,10},{10,1... | collective-permute-start | bytes 393224 | tf_op jit(solution)/shard_map/ppermute | solution.py:18
  64.5 0.9 collective-permute-done.1
  67.3 4.2 %scatter_fusion = f32[3,8,32,256]{3,2,1,0:T(8,128)S(1)} fusion(f32[3,8,32,256]{3,2,1,0:T(8,128)S(1)} %maximum_subtract_fusion, s32[48]{0:T(128)S(1)} %fusion.59, f32[48]{0:T(128)S(1)} %reshape.207), kind=kCustom, calls=%fused_computation.1 | custom fusion | flops 48 | bytes 1344 | tf_op jit(solution)/shard_map/scatter-add | solution.py:126
  71.5 1.7 %fusion.18 = (f32[1,8,32,256]{3,2,1,0:T(8,128)S(1)}, f32[1,8,32,256]{3,2,1,0:T(8,128)S(1)}, f32[1,8,32,256]{3,2,1,0:T(8,128)S(1)}) fusion(f32[7,32,256]{2,1,0:T(8,128)} %get-tuple-element.28, f32[1,32,256]{2,1,0:T(8,128)S(1)} %get-tuple-element.61, f32[8,32,255]{2,1,0:T(8,128)} %bitcast.192, f32[3,8,32,256]{3,2,1,0:T(8,128)S(1)} %fusion.1, ...), kind=kLoop, calls=%fused_computation.43 | loop fusion | flops 720896 | bytes 3127296 | tf_op jit(solution)/shard_map/stack | solution.py:57
  73.5 1.8 %multiply_reduce_fusion = (f32[8,32,256]{2,1,0:T(8,128)S(1)}, f32[3,8,32,256]{3,2,1,0:T(8,128)}, f32[3,8,32,256]{3,2,1,0:T(8,128)}) fusion(f32[3,8,32,256]{3,2,1,0:T(8,128)S(1)} %copy-done, f32[3,8,32,256]{3,2,1,0:T(8,128)S(1)} %copy-done.1, f32[8,32,256]{2,1,0:T(8,128)S(1)} %scatter_fusion.1, f32[3,8,32,256]{3,2,1,0:T(8,128)S(1)} %copy-done.18, ...), kind=kLoop, calls=%fused_computation.15 | loop fusion | flops 3866624 | bytes 7340032 | tf_op jit(solution)/shard_map/reduce_sum | solution.py:135
  76.5 1.1 copy.22
  77.7 55.9 %reduce-scatter.2.cloned.1.call-done = f32[1,32,256]{2,1,0:T(8,128)} async-done(((f32[16,32,256]{2,1,0:T(8,128)}), f32[1,32,256]{2,1,0:T(8,128)}) %reduce-scatter.2.cloned.1.call-update) | async-done | bytes 32784 | tf_op jit(solution)/shard_map/reduce_scatter | solution.py:139
  133.6 1.0 convolution_bitcast_fusion.2
  134.7 0.9 convolution_bitcast_fusion.1
  (123 shorter events, 16.4 us)
Async XLA Ops:
  7.2 6.9 %copy-start = (f32[3,8,32,256]{3,2,1,0:T(8,128)S(1)}, f32[3,8,32,256]{3,2,1,0:T(8,128)}, u32[]{:S(2)}) copy-start(f32[3,8,32,256]{3,2,1,0:T(8,128)} %param.14) | copy-start | bytes 2359300
  7.2 126.4 %reduce-scatter.2.cloned.1.call-start = ((), (), s32[]{:S(2)}) async-start(), calls=%async_computation.1 | async-start | bytes 557056 | tf_op jit(solution)/shard_map/reduce_scatter | solution.py:139
  8.8 47.3 %collective-permute-start = (f32[4,32,256]{2,1,0:T(8,128)}, f32[4,32,256]{2,1,0:T(8,128)S(1)}, u32[]{:S(2)}, u32[]{:S(2)}) collective-permute-start(f32[4,32,256]{2,1,0:T(8,128)} %pad_maximum_fusion), channel_id=1, source_target_pairs={{1,0},{2,1},{3,2},{4,3},{5,4},{6,5},{7,6},{8,7},{9,8},{10,9},{11,1... | collective-permute-start | bytes 393224 | tf_op jit(solution)/shard_map/ppermute | solution.py:18
  12.1 2.7 %copy-start.1 = (f32[3,8,32,256]{3,2,1,0:T(8,128)S(1)}, f32[3,8,32,256]{3,2,1,0:T(8,128)}, u32[]{:S(2)}) copy-start(f32[3,8,32,256]{3,2,1,0:T(8,128)} %param.18) | copy-start | bytes 2359300
  54.4 1.6 %copy-start.23 = (s32[48,1]{0,1:T(1,128)S(1)}, s32[48,1]{0,1:T(1,128)}, u32[]{:S(2)}) copy-start(s32[48,1]{0,1:T(1,128)} %reshape.193) | copy-start | bytes 580
  54.4 1.6 %copy-start.24 = (s32[48,1]{0,1:T(1,128)S(1)}, s32[48,1]{0,1:T(1,128)}, u32[]{:S(2)}) copy-start(s32[48,1]{0,1:T(1,128)} %tile.32) | copy-start | bytes 580
  54.4 1.6 %copy-start.25 = (s32[48,1]{0,1:T(1,128)S(1)}, s32[48,1]{0,1:T(1,128)}, u32[]{:S(2)}) copy-start(s32[48,1]{0,1:T(1,128)} %tile.30) | copy-start | bytes 580
  54.4 1.6 %copy-start.26 = (s32[48,1]{0,1:T(1,128)S(1)}, s32[48,1]{0,1:T(1,128)}, u32[]{:S(2)}) copy-start(s32[48,1]{0,1:T(1,128)} %tile.13) | copy-start | bytes 580
  54.4 1.7 %copy-start.14 = (f32[7,32,256]{2,1,0:T(8,128)S(1)}, f32[7,32,256]{2,1,0:T(8,128)}, u32[]{:S(2)}) copy-start(f32[7,32,256]{2,1,0:T(8,128)} %get-tuple-element.48) | copy-start | bytes 688132
  54.4 1.7 %copy-start.15 = (f32[7,32,256]{2,1,0:T(8,128)S(1)}, f32[7,32,256]{2,1,0:T(8,128)}, u32[]{:S(2)}) copy-start(f32[7,32,256]{2,1,0:T(8,128)} %get-tuple-element.49) | copy-start | bytes 688132
  58.3 13.2 %copy-start.2 = (f32[3,8,32,256]{3,2,1,0:T(8,128)}, f32[3,8,32,256]{3,2,1,0:T(8,128)S(1)}, u32[]{:S(2)}) copy-start(f32[3,8,32,256]{3,2,1,0:T(8,128)S(1)} %fusion.1) | copy-start | bytes 2359300
  59.2 1.4 copy-start.8
  59.2 1.5 %copy-start.9 = (f32[8,31,256]{2,1,0:T(8,128)S(1)}, f32[8,31,256]{2,1,0:T(8,128)}, u32[]{:S(2)}) copy-start(f32[8,31,256]{2,1,0:T(8,128)} %slice.273) | copy-start | bytes 761860
  59.2 1.5 %copy-start.12 = (f32[7,32,256]{2,1,0:T(8,128)S(1)}, f32[7,32,256]{2,1,0:T(8,128)}, u32[]{:S(2)}) copy-start(f32[7,32,256]{2,1,0:T(8,128)} %get-tuple-element.38) | copy-start | bytes 688132
  59.2 1.6 %copy-start.13 = (f32[7,32,256]{2,1,0:T(8,128)S(1)}, f32[7,32,256]{2,1,0:T(8,128)}, u32[]{:S(2)}) copy-start(f32[7,32,256]{2,1,0:T(8,128)} %get-tuple-element.39) | copy-start | bytes 688132
  62.1 3.4 %copy-start.3 = (f32[3,8,32,256]{3,2,1,0:T(8,128)}, f32[3,8,32,256]{3,2,1,0:T(8,128)S(1)}, u32[]{:S(2)}) copy-start(f32[3,8,32,256]{3,2,1,0:T(8,128)S(1)} %fusion) | copy-start | bytes 2359300
  62.2 3.2 %collective-permute-start.1 = (f32[4,32,256]{2,1,0:T(8,128)S(1)}, f32[4,32,256]{2,1,0:T(8,128)S(1)}, u32[]{:S(2)}, u32[]{:S(2)}) collective-permute-start(f32[4,32,256]{2,1,0:T(8,128)S(1)} %pad_maximum_fusion.1), channel_id=1, source_target_pairs={{0,1},{1,2},{2,3},{3,4},{4,5},{5,6},{6,7},{7,8},{8,9},{9,10},{10,1... | collective-permute-start | bytes 393224 | tf_op jit(solution)/shard_map/ppermute | solution.py:18
  65.5 1.4 %copy-start.17 = (f32[3,8,32,256]{3,2,1,0:T(8,128)S(1)}, f32[3,8,32,256]{3,2,1,0:T(8,128)}, u32[]{:S(2)}) copy-start(f32[3,8,32,256]{3,2,1,0:T(8,128)} %param.17) | copy-start | bytes 2359300
  71.5 1.8 %copy-start.5 = (f32[8,32,256]{2,1,0:T(8,128)S(1)}, f32[8,32,256]{2,1,0:T(8,128)}, u32[]{:S(2)}) copy-start(f32[8,32,256]{2,1,0:T(8,128)} %get-tuple-element.58) | copy-start | bytes 786436
  71.5 1.8 %copy-start.18 = (f32[3,8,32,256]{3,2,1,0:T(8,128)S(1)}, f32[3,8,32,256]{3,2,1,0:T(8,128)}, u32[]{:S(2)}) copy-start(f32[3,8,32,256]{3,2,1,0:T(8,128)} %param.20) | copy-start | bytes 2359300
  71.5 1.9 %copy-start.19 = (f32[3,8,32,256]{3,2,1,0:T(8,128)S(1)}, f32[3,8,32,256]{3,2,1,0:T(8,128)}, u32[]{:S(2)}) copy-start(f32[3,8,32,256]{3,2,1,0:T(8,128)} %param.21) | copy-start | bytes 2359300
  71.5 2.0 %copy-start.22 = (f32[8,32,256]{2,1,0:T(8,128)S(1)}, f32[8,32,256]{2,1,0:T(8,128)}, u32[]{:S(2)}) copy-start(f32[8,32,256]{2,1,0:T(8,128)} %get-tuple-element.57) | copy-start | bytes 786436
  77.6 56.0 %copy-start.34 = (f32[32]{0:T(128)S(1)}, f32[32]{0:T(128)}, u32[]{:S(2)}) copy-start(f32[32]{0:T(128)} %convert_reduce_fusion.1) | copy-start | bytes 388
  77.6 57.0 %copy-start.37 = (f32[256]{0:T(256)S(1)}, f32[256]{0:T(256)}, u32[]{:S(2)}) copy-start(f32[256]{0:T(256)} %convert_reduce_fusion) | copy-start | bytes 3076
  (17 other events, 14.4 us)
Sparse Core Ops, SparseCore 0:
  77.8 55.7 reduce-scatter.1
where the time goes:
time: 143 us; the launch traced here: 142 us
  waiting for transfers between devices  56.9 us (40%)
  blocking collectives  25.4 us (18%)
  local copies, waits for them, and re-layouts  22.6 us (16%)
  between operations  15.9 us (11%)
  other arithmetic  13.9 us (10%)
  matrix products  4.26 us (3%)
  starting transfers between devices  3.57 us (2%)
    reduce_scatter x1, waiting for transfers between devices, body(): lax.psum_scatter(returned, 'gx', scatter_dimension=0, tiled=True)  55.9 us
    all_gather x1, blocking collectives, body(): gathered = lax.all_gather(design, 'gx', axis=0, tiled=True)  25.4 us
    unnamed x76, local copies, waits for them, and re-layouts  7.77 us
    scatter-add x1, other arithmetic, body(): drive = jnp.zeros((3, depth, width_x, width_y), jnp.float32).at[comp, jnp...  4.22 us
    slice x8, local copies, waits for them, and re-layouts, ahead(): rest = lax.slice_in_dim(field, 1, count, axis=axis)  4.17 us
    ppermute x2, starting transfers between devices, passed_along(): return lax.ppermute(block, axis, route)  3.53 us
  transfers between devices with their start and end apart: 3, of which 2 were waited for; matrix products, arithmetic and copies ran while one was open for 12% of the time, Pallas kernels for 0%

commit v1 on v0

--- a/solution.py
+++ b/solution.py
@@ -2,6 +2,7 @@
 import jax.numpy as jnp
 from jax import lax
 from jax.sharding import PartitionSpec as P
+from jax.lax import axis_index, axis_size, ppermute
 
 DT = 0.5
 EPS_RANGE = 10.0
@@ -108,7 +109,18 @@
     )
     hf = update_h(e_forward, h_forward, upper[0:2])
     ha = update_h(e_adjoint, h_adjoint, upper[2:4])
-    gathered = lax.all_gather(design, "gx", axis=0, tiled=True)
+    how_many = axis_size("gx")
+    made = tuple(((src_i, (src_i + 1) % how_many) for src_i in range(how_many)))
+    b_now, extra = ([design], [design])
+    shelf = tuple(((src_i, (src_i - 1) % how_many) for src_i in range(how_many)))
+    for _ in range(how_many // 2):
+        field_out = ppermute(b_now[-1], "gx", made)
+        b_now.append(field_out)
+    for _ in range((how_many - 1) // 2):
+        block_out = ppermute(extra[-1], "gx", shelf)
+        extra.append(block_out)
+    shaped = jnp.concatenate([*b_now[::-1], *extra[1:]], axis=0)
+    gathered = jnp.roll(shaped, shift=(axis_index("gx") - how_many // 2) * design.shape[0], axis=0)
     slab = gathered.shape[0]
     planes = index * depth + jnp.arange(depth, dtype=jnp.int32) - start
     valid = ((planes >= 0) & (planes < slab)).astype(jnp.float32)

time: 143 us -> 170 us (1.19)
  starting transfers between devices: 3.57 us -> 35.1 us
  blocking collectives: 25.4 us -> 0 us
  local copies, waits for them, and re-layouts: 22.6 us -> 33.6 us
  waiting for transfers between devices: 56.9 us -> 64.4 us
    ppermute x0 -> x15, starting transfers between devices: none -> 31.7 us  [the longest x7 30 us: body(): block_out = ppermute(extra[-1], 'gx', shelf)]
    all_gather x1 -> x0, blocking collectives: 25.4 us -> none  [body(): gathered = lax.all_gather(design, 'gx', axis=0, tiled=True)]
    ppermute x0 -> x15, waiting for transfers between devices: none -> 10.3 us  [the longest x8 10.2 us: body(): field_out = ppermute(b_now[-1], 'gx', made)]
    unnamed x76 -> x117, local copies, waits for them, and re-layouts: 7.77 us -> 15.4 us
    reduce_scatter x1, waiting for transfers between devices: 55.9 us -> 54.1 us  [body(): lax.psum_scatter(returned, 'gx', scatter_dimension=0, tiled=True)]
    gather x1, local copies, waits for them, and re-layouts: 0.56 us -> 2.3 us  [body(): jnp.take(gathered, jnp.clip(planes, 0, slab - 1), axis=0)]
  transfers between devices with their start and end apart: 3 -> 18, of which waited for: 2 -> 7; matrix products, arithmetic and copies ran while one was open for 12% -> 18% of each run, Pallas kernels for 0% -> 0%
where the time goes in v1:
time: 170 us; the launch traced here: 168 us
  waiting for transfers between devices  64.4 us (38%)
  starting transfers between devices  35.1 us (21%)
  local copies, waits for them, and re-layouts  33.6 us (20%)
  between operations  16 us (9%)
  other arithmetic  14 us (8%)
  matrix products  5.13 us (3%)
    reduce_scatter x1, waiting for transfers between devices, body(): lax.psum_scatter(returned, 'gx', scatter_dimension=0, tiled=True)  54.1 us
    ppermute x7, starting transfers between devices, body(): block_out = ppermute(extra[-1], 'gx', shelf)  30 us
    unnamed x117, local copies, waits for them, and re-layouts  15.4 us
    ppermute x8, waiting for transfers between devices, body(): field_out = ppermute(b_now[-1], 'gx', made)  10.2 us
    scatter-add x1, other arithmetic, body(): drive = jnp.zeros((3, depth, width_x, width_y), jnp.float32).at[comp, jnp...  4.22 us
    slice x8, local copies, waits for them, and re-layouts, ahead(): rest = lax.slice_in_dim(field, 1, count, axis=axis)  4.16 us
  transfers between devices with their start and end apart: 18, of which 7 were waited for; matrix products, arithmetic and copies ran while one was open for 18% of the time, Pallas kernels for 0%

profile of v1, /device:TPU:0, one launch (start us, length us, event | category | flops | bytes accessed | tf_op | source)
XLA Modules:
  0.0 168.3 jit_solution(18215383341191028139)
XLA Ops:
  7.7 5.1 %collective-permute-start.8 = (f32[1,32,256]{2,1,0:T(8,128)}, f32[1,32,256]{2,1,0:T(8,128)S(1)}, u32[]{:S(2)}, u32[]{:S(2)}) collective-permute-start(f32[1,32,256]{2,1,0:T(8,128)} %param.22), channel_id=1, source_target_pairs={{0,15},{1,0},{2,1},{3,2},{4,3},{5,4},{6,5},{7,6},{8,7},{9,8},{10,9... | collective-permute-start | bytes 98312 | tf_op jit(solution)/shard_map/ppermute | solution.py:120
  14.3 1.4 collective-permute-start.15
  15.7 1.2 slice_bitcast_fusion.11
  23.3 1.1 collective-permute-start.1
  24.4 3.3 %collective-permute-start.9 = (f32[1,32,256]{2,1,0:T(8,128)S(1)}, f32[1,32,256]{2,1,0:T(8,128)}, u32[]{:S(2)}, u32[]{:S(2)}) collective-permute-start(f32[1,32,256]{2,1,0:T(8,128)S(1)} %collective-permute-done.8), channel_id=1, source_target_pairs={{0,15},{1,0},{2,1},{3,2},{4,3},{5,4},{6,5},{7,6},{8,7},{9,8},{10,9... | collective-permute-start | bytes 98312 | tf_op jit(solution)/shard_map/ppermute | solution.py:120
  27.8 1.7 %collective-permute-done.1 = f32[1,32,256]{2,1,0:T(8,128)} collective-permute-done((f32[1,32,256]{2,1,0:T(8,128)S(1)}, f32[1,32,256]{2,1,0:T(8,128)}, u32[]{:S(2)}, u32[]{:S(2)}) %collective-permute-start.1) | collective-permute-done | bytes 32800 | tf_op jit(solution)/shard_map/ppermute | solution.py:117
  29.5 4.4 %collective-permute-start.10 = (f32[1,32,256]{2,1,0:T(8,128)}, f32[1,32,256]{2,1,0:T(8,128)}, u32[]{:S(2)}, u32[]{:S(2)}) collective-permute-start(f32[1,32,256]{2,1,0:T(8,128)} %collective-permute-done.9), channel_id=1, source_target_pairs={{0,15},{1,0},{2,1},{3,2},{4,3},{5,4},{6,5},{7,6},{8,7},{9,8},{10,9... | collective-permute-start | bytes 98312 | tf_op jit(solution)/shard_map/ppermute | solution.py:120
  40.2 1.6 scatter_fusion.1
  42.6 4.4 %collective-permute-start.11 = (f32[1,32,256]{2,1,0:T(8,128)}, f32[1,32,256]{2,1,0:T(8,128)S(1)}, u32[]{:S(2)}, u32[]{:S(2)}) collective-permute-start(f32[1,32,256]{2,1,0:T(8,128)} %collective-permute-done.10), channel_id=1, source_target_pairs={{0,15},{1,0},{2,1},{3,2},{4,3},{5,4},{6,5},{7,6},{8,7},{9,8},{10,9... | collective-permute-start | bytes 98312 | tf_op jit(solution)/shard_map/ppermute | solution.py:120
  54.1 5.2 %collective-permute-done.4 = f32[1,32,256]{2,1,0:T(8,128)S(1)} collective-permute-done((f32[1,32,256]{2,1,0:T(8,128)S(1)}, f32[1,32,256]{2,1,0:T(8,128)S(1)}, u32[]{:S(2)}, u32[]{:S(2)}) %collective-permute-start.4) | collective-permute-done | bytes 32800 | tf_op jit(solution)/shard_map/ppermute | solution.py:117
  59.4 4.5 %collective-permute-start.12 = (f32[1,32,256]{2,1,0:T(8,128)S(1)}, f32[1,32,256]{2,1,0:T(8,128)S(1)}, u32[]{:S(2)}, u32[]{:S(2)}) collective-permute-start(f32[1,32,256]{2,1,0:T(8,128)S(1)} %collective-permute-done.11), channel_id=1, source_target_pairs={{0,15},{1,0},{2,1},{3,2},{4,3},{5,4},{6,5},{7,6},{8,7},{9,8},{10,9... | collective-permute-start | bytes 98312 | tf_op jit(solution)/shard_map/ppermute | solution.py:120
  63.9 1.5 collective-permute-done.5
  65.5 4.4 %collective-permute-start.13 = (f32[1,32,256]{2,1,0:T(8,128)S(1)}, f32[1,32,256]{2,1,0:T(8,128)S(1)}, u32[]{:S(2)}, u32[]{:S(2)}) collective-permute-start(f32[1,32,256]{2,1,0:T(8,128)S(1)} %collective-permute-done.12), channel_id=1, source_target_pairs={{0,15},{1,0},{2,1},{3,2},{4,3},{5,4},{6,5},{7,6},{8,7},{9,8},{10,9... | collective-permute-start | bytes 98312 | tf_op jit(solution)/shard_map/ppermute | solution.py:120
  69.9 1.5 collective-permute-done.6
  71.5 1.9 %collective-permute-start.16 = (f32[4,32,256]{2,1,0:T(8,128)S(1)}, f32[4,32,256]{2,1,0:T(8,128)}, u32[]{:S(2)}, u32[]{:S(2)}) collective-permute-start(f32[4,32,256]{2,1,0:T(8,128)S(1)} %pad_maximum_fusion.1), channel_id=1, source_target_pairs={{0,1},{1,2},{2,3},{3,4},{4,5},{5,6},{6,7},{7,8},{8,9},{9,10},{10,1... | collective-permute-start | bytes 393224 | tf_op jit(solution)/shard_map/ppermute | solution.py:19
  73.4 3.9 %collective-permute-start.14 = (f32[1,32,256]{2,1,0:T(8,128)S(1)}, f32[1,32,256]{2,1,0:T(8,128)S(1)}, u32[]{:S(2)}, u32[]{:S(2)}) collective-permute-start(f32[1,32,256]{2,1,0:T(8,128)S(1)} %collective-permute-done.13), channel_id=1, source_target_pairs={{0,15},{1,0},{2,1},{3,2},{4,3},{5,4},{6,5},{7,6},{8,7},{9,8},{10,9... | collective-permute-start | bytes 98312 | tf_op jit(solution)/shard_map/ppermute | solution.py:120
  86.2 2.3 %gather_fusion = f32[8,32,256]{2,1,0:T(8,128)} fusion(f32[16,32,256]{2,1,0:T(8,128)} %constant_dynamic-slice_fusion, s32[1024]{0:T(1024)S(1)} %pad_clamp_fusion), kind=kCustom, calls=%fused_computation | custom fusion | bytes 524320 | tf_op jit(solution)/shard_map/jit(_take)/gather | solution.py:127
  89.1 1.4 convolution_bitcast_fusion
  90.6 1.2 add_divide_fusion
  94.9 4.2 %scatter_fusion = f32[3,8,32,256]{3,2,1,0:T(8,128)S(1)} fusion(f32[3,8,32,256]{3,2,1,0:T(8,128)S(1)} %maximum_subtract_fusion, s32[48]{0:T(128)S(1)} %fusion.59, f32[48]{0:T(128)S(1)} %copy-done.33), kind=kCustom, calls=%fused_computation.1 | custom fusion | flops 48 | bytes 1344 | tf_op jit(solution)/shard_map/scatter-add | solution.py:138
  99.2 1.8 %fusion.18 = (f32[1,8,32,256]{3,2,1,0:T(8,128)S(1)}, f32[1,8,32,256]{3,2,1,0:T(8,128)S(1)}, f32[1,8,32,256]{3,2,1,0:T(8,128)S(1)}) fusion(f32[7,32,256]{2,1,0:T(8,128)} %get-tuple-element.28, f32[1,32,256]{2,1,0:T(8,128)S(1)} %get-tuple-element.61, f32[8,32,255]{2,1,0:T(8,128)} %bitcast.194, f32[3,8,32,256]{3,2,1,0:T(8,128)S(1)} %fusion.1, ...), kind=kLoop, calls=%fused_computation.43 | loop fusion | flops 720896 | bytes 3127296 | tf_op jit(solution)/shard_map/stack | solution.py:58
  101.1 1.8 %multiply_reduce_fusion = (f32[8,32,256]{2,1,0:T(8,128)S(1)}, f32[3,8,32,256]{3,2,1,0:T(8,128)}, f32[3,8,32,256]{3,2,1,0:T(8,128)}) fusion(f32[3,8,32,256]{3,2,1,0:T(8,128)S(1)} %copy-done, f32[3,8,32,256]{3,2,1,0:T(8,128)S(1)} %copy-done.1, f32[8,32,256]{2,1,0:T(8,128)S(1)} %scatter_fusion.1, f32[3,8,32,256]{3,2,1,0:T(8,128)S(1)} %copy-done.23, ...), kind=kLoop, calls=%fused_computation.15 | loop fusion | flops 3866624 | bytes 7340032 | tf_op jit(solution)/shard_map/reduce_sum | solution.py:147
  104.2 1.1 copy.22
  105.3 54.1 %reduce-scatter.2.cloned.1.call-done = f32[1,32,256]{2,1,0:T(8,128)} async-done(((f32[16,32,256]{2,1,0:T(8,128)}), f32[1,32,256]{2,1,0:T(8,128)}) %reduce-scatter.2.cloned.1.call-update) | async-done | bytes 32784 | tf_op jit(solution)/shard_map/reduce_scatter | solution.py:151
  (195 shorter events, 37.1 us)
Async XLA Ops:
  7.2 152.3 %reduce-scatter.2.cloned.1.call-start = ((), (), s32[]{:S(2)}) async-start(), calls=%async_computation.1 | async-start | bytes 557056 | tf_op jit(solution)/shard_map/reduce_scatter | solution.py:151
  7.2 16.1 %collective-permute-start = (f32[1,32,256]{2,1,0:T(8,128)}, f32[1,32,256]{2,1,0:T(8,128)S(1)}, u32[]{:S(2)}, u32[]{:S(2)}) collective-permute-start(f32[1,32,256]{2,1,0:T(8,128)} %param.22), channel_id=1, source_target_pairs={{0,1},{1,2},{2,3},{3,4},{4,5},{5,6},{6,7},{7,8},{8,9},{9,10},{10,1... | collective-permute-start | bytes 98312 | tf_op jit(solution)/shard_map/ppermute | solution.py:117
  7.7 16.7 %collective-permute-start.8 = (f32[1,32,256]{2,1,0:T(8,128)}, f32[1,32,256]{2,1,0:T(8,128)S(1)}, u32[]{:S(2)}, u32[]{:S(2)}) collective-permute-start(f32[1,32,256]{2,1,0:T(8,128)} %param.22), channel_id=1, source_target_pairs={{0,15},{1,0},{2,1},{3,2},{4,3},{5,4},{6,5},{7,6},{8,7},{9,8},{10,9... | collective-permute-start | bytes 98312 | tf_op jit(solution)/shard_map/ppermute | solution.py:120
  14.3 32.8 %collective-permute-start.15 = (f32[4,32,256]{2,1,0:T(8,128)}, f32[4,32,256]{2,1,0:T(8,128)S(1)}, u32[]{:S(2)}, u32[]{:S(2)}) collective-permute-start(f32[4,32,256]{2,1,0:T(8,128)} %pad_maximum_fusion), channel_id=1, source_target_pairs={{1,0},{2,1},{3,2},{4,3},{5,4},{6,5},{7,6},{8,7},{9,8},{10,9},{11,1... | collective-permute-start | bytes 393224 | tf_op jit(solution)/shard_map/ppermute | solution.py:19
  23.3 10.6 %copy-start.31 = (f32[1,32,256]{2,1,0:T(8,128)}, f32[1,32,256]{2,1,0:T(8,128)S(1)}, u32[]{:S(2)}) copy-start(f32[1,32,256]{2,1,0:T(8,128)S(1)} %collective-permute-done) | copy-start | bytes 98308
  23.3 6.1 %collective-permute-start.1 = (f32[1,32,256]{2,1,0:T(8,128)S(1)}, f32[1,32,256]{2,1,0:T(8,128)}, u32[]{:S(2)}, u32[]{:S(2)}) collective-permute-start(f32[1,32,256]{2,1,0:T(8,128)S(1)} %collective-permute-done), channel_id=1, source_target_pairs={{0,1},{1,2},{2,3},{3,4},{4,5},{5,6},{6,7},{7,8},{8,9},{9,10},{10,1... | collective-permute-start | bytes 98312 | tf_op jit(solution)/shard_map/ppermute | solution.py:117
  24.4 9.5 %copy-start.29 = (f32[1,32,256]{2,1,0:T(8,128)}, f32[1,32,256]{2,1,0:T(8,128)S(1)}, u32[]{:S(2)}) copy-start(f32[1,32,256]{2,1,0:T(8,128)S(1)} %collective-permute-done.8) | copy-start | bytes 98308
  24.4 5.0 %collective-permute-start.9 = (f32[1,32,256]{2,1,0:T(8,128)S(1)}, f32[1,32,256]{2,1,0:T(8,128)}, u32[]{:S(2)}, u32[]{:S(2)}) collective-permute-start(f32[1,32,256]{2,1,0:T(8,128)S(1)} %collective-permute-done.8), channel_id=1, source_target_pairs={{0,15},{1,0},{2,1},{3,2},{4,3},{5,4},{6,5},{7,6},{8,7},{9,8},{10,9... | collective-permute-start | bytes 98312 | tf_op jit(solution)/shard_map/ppermute | solution.py:120
  29.5 13.2 %collective-permute-start.2 = (f32[1,32,256]{2,1,0:T(8,128)}, f32[1,32,256]{2,1,0:T(8,128)}, u32[]{:S(2)}, u32[]{:S(2)}) collective-permute-start(f32[1,32,256]{2,1,0:T(8,128)} %collective-permute-done.1), channel_id=1, source_target_pairs={{0,1},{1,2},{2,3},{3,4},{4,5},{5,6},{6,7},{7,8},{8,9},{9,10},{10,1... | collective-permute-start | bytes 98312 | tf_op jit(solution)/shard_map/ppermute | solution.py:117
  29.5 13.2 %collective-permute-start.10 = (f32[1,32,256]{2,1,0:T(8,128)}, f32[1,32,256]{2,1,0:T(8,128)}, u32[]{:S(2)}, u32[]{:S(2)}) collective-permute-start(f32[1,32,256]{2,1,0:T(8,128)} %collective-permute-done.9), channel_id=1, source_target_pairs={{0,15},{1,0},{2,1},{3,2},{4,3},{5,4},{6,5},{7,6},{8,7},{9,8},{10,9... | collective-permute-start | bytes 98312 | tf_op jit(solution)/shard_map/ppermute | solution.py:120
  40.2 6.9 %copy-start.17 = (f32[7,32,256]{2,1,0:T(8,128)S(1)}, f32[7,32,256]{2,1,0:T(8,128)}, u32[]{:S(2)}) copy-start(f32[7,32,256]{2,1,0:T(8,128)} %get-tuple-element.38) | copy-start | bytes 688132
  40.2 6.9 %copy-start.18 = (f32[7,32,256]{2,1,0:T(8,128)S(1)}, f32[7,32,256]{2,1,0:T(8,128)}, u32[]{:S(2)}) copy-start(f32[7,32,256]{2,1,0:T(8,128)} %get-tuple-element.39) | copy-start | bytes 688132
  42.6 10.7 %collective-permute-start.3 = (f32[1,32,256]{2,1,0:T(8,128)}, f32[1,32,256]{2,1,0:T(8,128)S(1)}, u32[]{:S(2)}, u32[]{:S(2)}) collective-permute-start(f32[1,32,256]{2,1,0:T(8,128)} %collective-permute-done.2), channel_id=1, source_target_pairs={{0,1},{1,2},{2,3},{3,4},{4,5},{5,6},{6,7},{7,8},{8,9},{9,10},{10,1... | collective-permute-start | bytes 98312 | tf_op jit(solution)/shard_map/ppermute | solution.py:117
  42.6 16.8 %collective-permute-start.11 = (f32[1,32,256]{2,1,0:T(8,128)}, f32[1,32,256]{2,1,0:T(8,128)S(1)}, u32[]{:S(2)}, u32[]{:S(2)}) collective-permute-start(f32[1,32,256]{2,1,0:T(8,128)} %collective-permute-done.10), channel_id=1, source_target_pairs={{0,15},{1,0},{2,1},{3,2},{4,3},{5,4},{6,5},{7,6},{8,7},{9,8},{10,9... | collective-permute-start | bytes 98312 | tf_op jit(solution)/shard_map/ppermute | solution.py:120
  48.4 44.4 %copy-start.2 = (f32[3,8,32,256]{3,2,1,0:T(8,128)}, f32[3,8,32,256]{3,2,1,0:T(8,128)S(1)}, u32[]{:S(2)}) copy-start(f32[3,8,32,256]{3,2,1,0:T(8,128)S(1)} %fusion) | copy-start | bytes 2359300
  51.5 47.6 %copy-start.3 = (f32[3,8,32,256]{3,2,1,0:T(8,128)}, f32[3,8,32,256]{3,2,1,0:T(8,128)S(1)}, u32[]{:S(2)}) copy-start(f32[3,8,32,256]{3,2,1,0:T(8,128)S(1)} %fusion.1) | copy-start | bytes 2359300
  53.3 6.0 %collective-permute-start.4 = (f32[1,32,256]{2,1,0:T(8,128)S(1)}, f32[1,32,256]{2,1,0:T(8,128)S(1)}, u32[]{:S(2)}, u32[]{:S(2)}) collective-permute-start(f32[1,32,256]{2,1,0:T(8,128)S(1)} %collective-permute-done.3), channel_id=1, source_target_pairs={{0,1},{1,2},{2,3},{3,4},{4,5},{5,6},{6,7},{7,8},{8,9},{9,10},{10,1... | collective-permute-start | bytes 98312 | tf_op jit(solution)/shard_map/ppermute | solution.py:117
  59.4 6.0 %collective-permute-start.5 = (f32[1,32,256]{2,1,0:T(8,128)S(1)}, f32[1,32,256]{2,1,0:T(8,128)S(1)}, u32[]{:S(2)}, u32[]{:S(2)}) collective-permute-start(f32[1,32,256]{2,1,0:T(8,128)S(1)} %collective-permute-done.4), channel_id=1, source_target_pairs={{0,1},{1,2},{2,3},{3,4},{4,5},{5,6},{6,7},{7,8},{8,9},{9,10},{10,1... | collective-permute-start | bytes 98312 | tf_op jit(solution)/shard_map/ppermute | solution.py:117
  59.4 6.1 %collective-permute-start.12 = (f32[1,32,256]{2,1,0:T(8,128)S(1)}, f32[1,32,256]{2,1,0:T(8,128)S(1)}, u32[]{:S(2)}, u32[]{:S(2)}) collective-permute-start(f32[1,32,256]{2,1,0:T(8,128)S(1)} %collective-permute-done.11), channel_id=1, source_target_pairs={{0,15},{1,0},{2,1},{3,2},{4,3},{5,4},{6,5},{7,6},{8,7},{9,8},{10,9... | collective-permute-start | bytes 98312 | tf_op jit(solution)/shard_map/ppermute | solution.py:120
  65.4 6.0 %collective-permute-start.6 = (f32[1,32,256]{2,1,0:T(8,128)S(1)}, f32[1,32,256]{2,1,0:T(8,128)S(1)}, u32[]{:S(2)}, u32[]{:S(2)}) collective-permute-start(f32[1,32,256]{2,1,0:T(8,128)S(1)} %collective-permute-done.5), channel_id=1, source_target_pairs={{0,1},{1,2},{2,3},{3,4},{4,5},{5,6},{6,7},{7,8},{8,9},{9,10},{10,1... | collective-permute-start | bytes 98312 | tf_op jit(solution)/shard_map/ppermute | solution.py:117
  65.5 7.9 %collective-permute-start.13 = (f32[1,32,256]{2,1,0:T(8,128)S(1)}, f32[1,32,256]{2,1,0:T(8,128)S(1)}, u32[]{:S(2)}, u32[]{:S(2)}) collective-permute-start(f32[1,32,256]{2,1,0:T(8,128)S(1)} %collective-permute-done.12), channel_id=1, source_target_pairs={{0,15},{1,0},{2,1},{3,2},{4,3},{5,4},{6,5},{7,6},{8,7},{9,8},{10,9... | collective-permute-start | bytes 98312 | tf_op jit(solution)/shard_map/ppermute | solution.py:120
  71.4 6.0 %collective-permute-start.7 = (f32[1,32,256]{2,1,0:T(8,128)S(1)}, f32[1,32,256]{2,1,0:T(8,128)S(1)}, u32[]{:S(2)}, u32[]{:S(2)}) collective-permute-start(f32[1,32,256]{2,1,0:T(8,128)S(1)} %collective-permute-done.6), channel_id=1, source_target_pairs={{0,1},{1,2},{2,3},{3,4},{4,5},{5,6},{6,7},{7,8},{8,9},{9,10},{10,1... | collective-permute-start | bytes 98312 | tf_op jit(solution)/shard_map/ppermute | solution.py:117
  71.5 20.3 %collective-permute-start.16 = (f32[4,32,256]{2,1,0:T(8,128)S(1)}, f32[4,32,256]{2,1,0:T(8,128)}, u32[]{:S(2)}, u32[]{:S(2)}) collective-permute-start(f32[4,32,256]{2,1,0:T(8,128)S(1)} %pad_maximum_fusion.1), channel_id=1, source_target_pairs={{0,1},{1,2},{2,3},{3,4},{4,5},{5,6},{6,7},{7,8},{8,9},{9,10},{10,1... | collective-permute-start | bytes 393224 | tf_op jit(solution)/shard_map/ppermute | solution.py:19
  73.4 8.7 %collective-permute-start.14 = (f32[1,32,256]{2,1,0:T(8,128)S(1)}, f32[1,32,256]{2,1,0:T(8,128)S(1)}, u32[]{:S(2)}, u32[]{:S(2)}) collective-permute-start(f32[1,32,256]{2,1,0:T(8,128)S(1)} %collective-permute-done.13), channel_id=1, source_target_pairs={{0,15},{1,0},{2,1},{3,2},{4,3},{5,4},{6,5},{7,6},{8,7},{9,8},{10,9... | collective-permute-start | bytes 98312 | tf_op jit(solution)/shard_map/ppermute | solution.py:120
  (37 other events, 54.2 us)
Sparse Core Ops, SparseCore 0:
  105.4 53.9 reduce-scatter.1
